TPU v7x, 256 devices: a whole 4x4x8 slice. The times are simulated.
256 devices in a mesh: seq: 32 (over x, z), tp: 8 (over y, core).
Axes of the slice: x: 4, y: 4, z: 8, core: 2. Of those that a mesh axis runs over, the one named last changes fastest.
Arguments:
- tokens: bfloat16 [32768, 2048], P('seq', 'tp'), may hold values from -6 to 6
- w_inner: bfloat16 [2048, 2, 4096], P('seq', None, 'tp'), may hold values from -0.125 to 0.125
- w_states: bfloat16 [2048, 256], P('seq'), may hold values from -0.125 to 0.125
- w_step: bfloat16 [2048, 64], P('seq', 'tp'), may hold values from -0.125 to 0.125
- conv_inner: float32 [4, 4096], P(None, 'tp'), may hold values from -3 to 3
- conv_states: float32 [4, 256], replicated, may hold values from -3 to 3
- decay_rate: float32 [64], P('tp'), may hold values from 0 to 1, as said below
- step_bias: float32 [64], P('tp'), may hold values from -1 to 0.5
- skip_gain: float32 [64], P('tp'), may hold values from 0.5 to 1.5
- norm_gain: float32 [4096], P('tp'), may hold values from 0.5 to 1.5
- w_output: bfloat16 [4096, 2048], P('tp', 'seq'), may hold values from -0.09375 to 0.09375
- block_owner: int32 [128], replicated, may hold values from 0 to 19, as said below
- lengths: int32 [20], replicated, may hold values from 1 to 16384, as said below
Outputs:
- mixed: bfloat16 [32768, 2048], P('seq', 'tp')
Inputs may be any that keep to these rules, and one draw needn't show every extreme that they name: `block_owner`: each prompt's blocks are consecutive, prompt r has ceil(lengths[r] / 256) of them, and the prompts follow one another in an order drawn afresh; one prompt has 64 blocks and is neither the first nor the last in that order. `lengths`: one prompt has exactly 16384 tokens. `decay_rate`: Positive.
All inputs are finite; a program needn't handle non-finite values.
Results may differ from a plain program's by a relative error of at most 0.0075.
Values may be sent and summed in bfloat16 or wider, within the bound.
No kernel may reach another device: no remote copies, remote signals or barrier semaphores. Data moves between devices by JAX's collectives and lax.ppermute only.
A program may use at most 64 MiB of HBM per device.

v0:
```python
import jax
import jax.numpy as jnp
from jax import lax
from jax.sharding import PartitionSpec as P

BLOCK = 256


def passed_along(value, axis, by):
    count = lax.axis_size(axis)
    pairs = [(i, i + by) for i in range(count) if 0 <= i + by < count]
    return lax.ppermute(value, axis, pairs)


def convolve(values, edge_rows, weights, in_block, carry_on):
    lag_rows = weights.shape[0] - 1
    row_total = values.shape[0]
    widened = jnp.concatenate([edge_rows, values], axis=0).astype(jnp.float32)
    total = jnp.zeros(values.shape, jnp.float32)
    for offset in range(weights.shape[0]):
        shifted = widened[lag_rows - offset : lag_rows - offset + row_total]
        keeping = (in_block >= offset) | carry_on
        total = total + jnp.where(keeping[:, None], shifted, 0.0) * weights[offset]
    return jax.nn.silu(total).astype(jnp.bfloat16)


def on_device(
    tokens,
    w_inner,
    w_states,
    w_step,
    conv_inner,
    conv_states,
    decay_rate,
    step_bias,
    skip_gain,
    norm_gain,
    w_output,
    block_owner,
    lengths,
):
    row_count = tokens.shape[0]
    local_blocks = row_count // BLOCK
    total_blocks = block_owner.shape[0]
    heads_here = w_step.shape[1]
    inner_here = w_inner.shape[2]
    state_size = w_states.shape[1] // 2
    head_size = inner_here // heads_here
    lag_rows = conv_inner.shape[0] - 1
    block_ids = jnp.arange(total_blocks, dtype=jnp.int32)
    same_owner = block_owner[:, None] == block_owner[None, :]
    first_block = jnp.min(jnp.where(same_owner, block_ids[None, :], total_blocks), axis=1)
    starting = (first_block == block_ids).astype(jnp.int32)
    request_ids = jnp.arange(lengths.shape[0], dtype=jnp.int32)
    own_length = jnp.sum(
        jnp.where(block_owner[:, None] == request_ids[None, :], lengths[None, :], 0), axis=1
    )
    valid_rows = jnp.clip(own_length - (block_ids - first_block) * BLOCK, 0, BLOCK)
    seq_index = lax.axis_index("seq")
    local_start = lax.dynamic_slice_in_dim(starting, seq_index * local_blocks, local_blocks)
    local_valid = lax.dynamic_slice_in_dim(valid_rows, seq_index * local_blocks, local_blocks)
    in_block = jnp.arange(row_count, dtype=jnp.int32) % BLOCK
    carry_on = jnp.repeat(local_start == 0, BLOCK)
    whole = lax.all_gather(tokens, "tp", axis=1, tiled=True)
    pieces = (
        lax.all_gather(w_inner, "seq", axis=0, tiled=True),
        lax.all_gather(w_states, "seq", axis=0, tiled=True),
        lax.all_gather(w_step, "seq", axis=0, tiled=True),
    )
    count = pieces[0].shape[0]
    inner_sum = jnp.dot(
        whole, pieces[0].reshape(count, 2 * inner_here), preferred_element_type=jnp.float32
    )
    states_sum = jnp.dot(whole, pieces[1], preferred_element_type=jnp.float32)
    step_sum = jnp.dot(whole, pieces[2], preferred_element_type=jnp.float32)
    projected = inner_sum.astype(jnp.bfloat16)
    gate_in = projected[:, :inner_here]
    x_in = projected[:, inner_here:]
    bc_in = states_sum.astype(jnp.bfloat16)
    step_raw = step_sum.astype(jnp.bfloat16)
    edge_inner, edge_states = passed_along(
        (x_in[row_count - lag_rows :], bc_in[row_count - lag_rows :]), "seq", 1
    )
    x_conv = convolve(x_in, edge_inner, conv_inner, in_block, carry_on)
    bc_conv = convolve(bc_in, edge_states, conv_states, in_block, carry_on)
    step_size = jax.nn.softplus(step_raw.astype(jnp.float32) + step_bias)
    log_decay = -decay_rate * step_size
    x_heads = x_conv.reshape(local_blocks, BLOCK, heads_here, head_size)
    b_rows = bc_conv[:, :state_size].reshape(local_blocks, BLOCK, state_size)
    c_rows = bc_conv[:, state_size:].reshape(local_blocks, BLOCK, state_size)
    step_blocks = step_size.reshape(local_blocks, BLOCK, heads_here)
    cumulative = jnp.cumsum(log_decay.reshape(local_blocks, BLOCK, heads_here), axis=1)
    causal = jnp.arange(BLOCK)[:, None] >= jnp.arange(BLOCK)[None, :]
    spread = cumulative[:, :, None, :] - cumulative[:, None, :, :]
    decays = jnp.exp(jnp.where(causal[None, :, :, None], spread, -jnp.inf))
    intersection = jnp.einsum("cin,cjn->cij", c_rows, b_rows, preferred_element_type=jnp.float32)
    mixing = (decays * intersection[:, :, :, None] * step_blocks[:, None, :, :]).astype(
        jnp.bfloat16
    )
    y_inner = jnp.einsum("cijh,cjhp->cihp", mixing, x_heads, preferred_element_type=jnp.float32)
    final_log = cumulative[:, -1, :]
    tail_weight = jnp.exp(final_log[:, None, :] - cumulative) * step_blocks
    weighted_b = (tail_weight[:, :, :, None] * b_rows.astype(jnp.float32)[:, :, None, :]).astype(
        jnp.bfloat16
    )
    fresh = jnp.einsum("cjhn,cjhp->chnp", weighted_b, x_heads, preferred_element_type=jnp.float32)
    keep_flag = jnp.where(local_start == 1, 0.0, 1.0).astype(jnp.float32)
    block_gain_each = jnp.exp(final_log) * keep_flag[:, None]

    def fold_block(carry, item):
        gain_now, fresh_now = item
        return ((carry[0] * gain_now, gain_now[:, None, None] * carry[1] + fresh_now), None)

    zero_state = jnp.zeros((heads_here, state_size, head_size), jnp.float32)
    unit_gain = jnp.ones((heads_here,), jnp.float32)
    (block_gain, block_state), _ = lax.scan(
        fold_block, (unit_gain, zero_state), (block_gain_each, fresh)
    )

    def relay(iteration, entering_now):
        return passed_along(block_gain[:, None, None] * entering_now + block_state, "seq", 1)

    entering = lax.fori_loop(0, lax.axis_size("seq") - 1, relay, zero_state)

    def pass_block(previous, item):
        log_now, keep_now, fresh_now = item
        incoming = previous * keep_now
        return (jnp.exp(log_now)[:, None, None] * incoming + fresh_now, incoming)

    _, incoming_all = lax.scan(pass_block, entering, (final_log, keep_flag, fresh))
    incoming_half = incoming_all.astype(jnp.bfloat16)
    y_carry = jnp.exp(cumulative)[:, :, :, None] * jnp.einsum(
        "cin,chnp->cihp", c_rows, incoming_half, preferred_element_type=jnp.float32
    )
    y_total = (y_inner + y_carry).reshape(row_count, inner_here) + jnp.repeat(skip_gain, head_size)[
        None, :
    ] * x_conv.astype(jnp.float32)
    gated = y_total * jax.nn.silu(gate_in.astype(jnp.float32))
    squares = lax.psum(jnp.sum(gated * gated, axis=1), "tp")
    square_mean = squares / (inner_here * lax.axis_size("tp"))
    normed = (gated * lax.rsqrt(square_mean + 1e-05)[:, None] * norm_gain).astype(jnp.bfloat16)
    partial_out = jnp.dot(
        normed,
        lax.all_gather(w_output, "seq", axis=1, tiled=True),
        preferred_element_type=jnp.float32,
    )
    summed = lax.psum_scatter(partial_out, "tp", scatter_dimension=1, tiled=True)
    live = in_block < jnp.repeat(local_valid, BLOCK)
    return jnp.where(live[:, None], summed, 0.0).astype(jnp.bfloat16)


def solution(mesh):
    return jax.shard_map(
        on_device,
        mesh=mesh,
        in_specs=(
            P("seq", "tp"),
            P("seq", None, "tp"),
            P("seq", None),
            P("seq", "tp"),
            P(None, "tp"),
            P(),
            P("tp"),
            P("tp"),
            P("tp"),
            P("tp"),
            P("tp", "seq"),
            P(),
            P(),
        ),
        out_specs=P("seq", "tp"),
        check_vma=False,
    )
```

profile of v0, /device:TPU:1, one launch (start us, length us, event | category | flops | bytes accessed | tf_op | source)
XLA Modules:
  0.0 875.8 jit_solution(9368195072958447139)
XLA Ops:
  13.4 41.9 %all-gather = bf16[32,64,8]{1,2,0:T(8,128)(2,1)S(1)} all-gather(bf16[1,64,8]{1,2,0:T(8,128)(2,1)} %bitcast.99), channel_id=1, replica_groups=mesh['seq'=32,'tp'=8] {'seq'}, dimensions={0}, use_global_device_ids=true | all-gather | bytes 33792 | tf_op jit(solution)/shard_map/all_gather | solution.py:68
  57.5 27.5 %all-gather.10.cloned.1.call-done = bf16[2048,256]{1,0:T(8,128)(2,1)} async-done(((bf16[64,256]{1,0:T(8,128)(2,1)}), bf16[2048,256]{1,0:T(8,128)(2,1)}) %all-gather.10.cloned.1.call-update) | async-done | bytes 1048592 | tf_op jit(solution)/shard_map/all_gather | solution.py:67
  85.0 42.9 %all-gather.6.cloned.1.call-done = bf16[1024,2048]{1,0:T(8,128)(2,1)} async-done(((bf16[1024,256]{1,0:T(8,128)(2,1)}), bf16[1024,2048]{1,0:T(8,128)(2,1)}) %all-gather.6.cloned.1.call-update) | async-done | bytes 4194320 | tf_op jit(solution)/shard_map/all_gather | solution.py:64
  141.9 67.3 %all-gather.8.cloned.1.call-done = bf16[2048,2,512]{2,1,0:T(2,128)(2,1)} async-done(((bf16[64,2,512]{2,1,0:T(2,128)(2,1)}), bf16[2048,2,512]{2,1,0:T(2,128)(2,1)}) %all-gather.8.cloned.1.call-update) | async-done | bytes 4194320 | tf_op jit(solution)/shard_map/all_gather | solution.py:66
  245.5 454.9 %while.35 = (s32[]{:T(128)}, f32[8,128,64]{2,1,0:T(8,128)S(1)}, f32[8]{0:T(128)S(1)}, f32[8,128,64]{2,1,0:T(8,128)S(1)}, s32[]{:T(128)}) while((s32[]{:T(128)}, f32[8,128,64]{2,1,0:T(8,128)S(1)}, f32[8]{0:T(128)S(1)}, f32[8,128,64]{2,1,0:T(8,128)S(1)}, s32[]{:T(128)}) %tuple.77), condition=%wide.region_7.8_spmd, body=%wide.region_6.7_spmd.sunk | while | flops 131074 | bytes 1835141 | solution.py:123
  262.2 9.9 %collective-permute-done = f32[8,128,64]{2,1,0:T(8,128)S(1)} collective-permute-done((f32[8,128,64]{2,1,0:T(8,128)}, f32[8,128,64]{2,1,0:T(8,128)S(1)}, u32[]{:S(2)}, u32[]{:S(2)}) %collective-permute-start) | collective-permute-done | bytes 262176 | tf_op jit(solution)/shard_map/while/body/eval_jaxpr/ppermute | solution.py:12
  277.4 11.2 %collective-permute-done = f32[8,128,64]{2,1,0:T(8,128)S(1)} collective-permute-done((f32[8,128,64]{2,1,0:T(8,128)}, f32[8,128,64]{2,1,0:T(8,128)S(1)}, u32[]{:S(2)}, u32[]{:S(2)}) %collective-permute-start) | collective-permute-done | bytes 262176 | tf_op jit(solution)/shard_map/while/body/eval_jaxpr/ppermute | solution.py:12
  329.6 9.5 %collective-permute-done = f32[8,128,64]{2,1,0:T(8,128)S(1)} collective-permute-done((f32[8,128,64]{2,1,0:T(8,128)}, f32[8,128,64]{2,1,0:T(8,128)S(1)}, u32[]{:S(2)}, u32[]{:S(2)}) %collective-permute-start) | collective-permute-done | bytes 262176 | tf_op jit(solution)/shard_map/while/body/eval_jaxpr/ppermute | solution.py:12
  343.8 10.7 %collective-permute-done = f32[8,128,64]{2,1,0:T(8,128)S(1)} collective-permute-done((f32[8,128,64]{2,1,0:T(8,128)}, f32[8,128,64]{2,1,0:T(8,128)S(1)}, u32[]{:S(2)}, u32[]{:S(2)}) %collective-permute-start) | collective-permute-done | bytes 262176 | tf_op jit(solution)/shard_map/while/body/eval_jaxpr/ppermute | solution.py:12
  359.2 11.8 %collective-permute-done = f32[8,128,64]{2,1,0:T(8,128)S(1)} collective-permute-done((f32[8,128,64]{2,1,0:T(8,128)}, f32[8,128,64]{2,1,0:T(8,128)S(1)}, u32[]{:S(2)}, u32[]{:S(2)}) %collective-permute-start) | collective-permute-done | bytes 262176 | tf_op jit(solution)/shard_map/while/body/eval_jaxpr/ppermute | solution.py:12
  376.7 12.0 %collective-permute-done = f32[8,128,64]{2,1,0:T(8,128)S(1)} collective-permute-done((f32[8,128,64]{2,1,0:T(8,128)}, f32[8,128,64]{2,1,0:T(8,128)S(1)}, u32[]{:S(2)}, u32[]{:S(2)}) %collective-permute-start) | collective-permute-done | bytes 262176 | tf_op jit(solution)/shard_map/while/body/eval_jaxpr/ppermute | solution.py:12
  394.9 10.9 %collective-permute-done = f32[8,128,64]{2,1,0:T(8,128)S(1)} collective-permute-done((f32[8,128,64]{2,1,0:T(8,128)}, f32[8,128,64]{2,1,0:T(8,128)S(1)}, u32[]{:S(2)}, u32[]{:S(2)}) %collective-permute-start) | collective-permute-done | bytes 262176 | tf_op jit(solution)/shard_map/while/body/eval_jaxpr/ppermute | solution.py:12
  411.4 9.8 %collective-permute-done = f32[8,128,64]{2,1,0:T(8,128)S(1)} collective-permute-done((f32[8,128,64]{2,1,0:T(8,128)}, f32[8,128,64]{2,1,0:T(8,128)S(1)}, u32[]{:S(2)}, u32[]{:S(2)}) %collective-permute-start) | collective-permute-done | bytes 262176 | tf_op jit(solution)/shard_map/while/body/eval_jaxpr/ppermute | solution.py:12
  426.1 8.6 collective-permute-done
  533.0 8.7 collective-permute-done
  548.7 9.5 %collective-permute-done = f32[8,128,64]{2,1,0:T(8,128)S(1)} collective-permute-done((f32[8,128,64]{2,1,0:T(8,128)}, f32[8,128,64]{2,1,0:T(8,128)S(1)}, u32[]{:S(2)}, u32[]{:S(2)}) %collective-permute-start) | collective-permute-done | bytes 262176 | tf_op jit(solution)/shard_map/while/body/eval_jaxpr/ppermute | solution.py:12
  566.1 10.6 %collective-permute-done = f32[8,128,64]{2,1,0:T(8,128)S(1)} collective-permute-done((f32[8,128,64]{2,1,0:T(8,128)}, f32[8,128,64]{2,1,0:T(8,128)S(1)}, u32[]{:S(2)}, u32[]{:S(2)}) %collective-permute-start) | collective-permute-done | bytes 262176 | tf_op jit(solution)/shard_map/while/body/eval_jaxpr/ppermute | solution.py:12
  585.3 11.8 %collective-permute-done = f32[8,128,64]{2,1,0:T(8,128)S(1)} collective-permute-done((f32[8,128,64]{2,1,0:T(8,128)}, f32[8,128,64]{2,1,0:T(8,128)S(1)}, u32[]{:S(2)}, u32[]{:S(2)}) %collective-permute-start) | collective-permute-done | bytes 262176 | tf_op jit(solution)/shard_map/while/body/eval_jaxpr/ppermute | solution.py:12
  605.7 11.1 %collective-permute-done = f32[8,128,64]{2,1,0:T(8,128)S(1)} collective-permute-done((f32[8,128,64]{2,1,0:T(8,128)}, f32[8,128,64]{2,1,0:T(8,128)S(1)}, u32[]{:S(2)}, u32[]{:S(2)}) %collective-permute-start) | collective-permute-done | bytes 262176 | tf_op jit(solution)/shard_map/while/body/eval_jaxpr/ppermute | solution.py:12
  624.5 9.9 %collective-permute-done = f32[8,128,64]{2,1,0:T(8,128)S(1)} collective-permute-done((f32[8,128,64]{2,1,0:T(8,128)}, f32[8,128,64]{2,1,0:T(8,128)S(1)}, u32[]{:S(2)}, u32[]{:S(2)}) %collective-permute-start) | collective-permute-done | bytes 262176 | tf_op jit(solution)/shard_map/while/body/eval_jaxpr/ppermute | solution.py:12
  641.4 8.8 %collective-permute-done = f32[8,128,64]{2,1,0:T(8,128)S(1)} collective-permute-done((f32[8,128,64]{2,1,0:T(8,128)}, f32[8,128,64]{2,1,0:T(8,128)S(1)}, u32[]{:S(2)}, u32[]{:S(2)}) %collective-permute-start) | collective-permute-done | bytes 262176 | tf_op jit(solution)/shard_map/while/body/eval_jaxpr/ppermute | solution.py:12
  700.5 15.3 %while.36 = (s32[]{:T(128)}, f32[8,128,64]{2,1,0:T(8,128)S(1)}, bf16[4,8,128,64]{3,2,1,0:T(8,128)(2,1)}, f32[4,8]{1,0:T(4,128)S(1)}, f32[4]{0:T(128)S(1)}, /*index=5*/f32[4,8,128,64]{3,2,1,0:T(8,128)}, s32[]{:T(128)}) while((s32[]{:T(128)}, f32[8,128,64]{2,1,0:T(8,128)S(1)}, bf16[4,8,128,64]{3,2,1,0:T(8,128)(2,1)}, f32[4,8]{1,0:T(4,128)S(1)}, ...), condition=%wide.region_9.10_spmd, body=%wide.region_8.9_spmd.sunk | while | flops 262146 | bytes 1574085 | solution.py:130
  737.1 48.3 %psum.7 = f32[1024]{0:T(1024)S(1)} all-reduce(f32[1024]{0:T(1024)S(1)} %get-tuple-element.196), channel_id=1, replica_groups=mesh['seq'=32,'tp'=8] {'tp'}, use_global_device_ids=true, to_apply=%region_11.12 | all-reduce | flops 1024 | bytes 8192 | tf_op jit(solution)/shard_map/psum | solution.py:139
  794.3 72.8 %reduce-scatter.2.cloned.1.call-done = f32[1024,256]{1,0:T(8,128)} async-done(((f32[1024,2048]{1,0:T(8,128)}), f32[1024,256]{1,0:T(8,128)}) %reduce-scatter.2.cloned.1.call-update) | async-done | bytes 1048592 | tf_op jit(solution)/shard_map/reduce_scatter | solution.py:147
  (220 shorter events, 403.5 us)
Async XLA Ops:
  6.5 78.4 %all-gather.10.cloned.1.call-start = ((), (), s32[]{:S(2)}) async-start(), calls=%async_computation.3 | async-start | bytes 1081344 | tf_op jit(solution)/shard_map/all_gather | solution.py:67
  7.3 120.7 %all-gather.6.cloned.1.call-start = ((), (), s32[]{:S(2)}) async-start(), calls=%async_computation.1 | async-start | bytes 4718592 | tf_op jit(solution)/shard_map/all_gather | solution.py:64
  8.0 201.3 %all-gather.8.cloned.1.call-start = ((), (), s32[]{:S(2)}) async-start(), calls=%async_computation.2 | async-start | bytes 4325376 | tf_op jit(solution)/shard_map/all_gather | solution.py:66
  8.7 776.7 %all-gather.12.cloned.1.call-start = ((), (), s32[]{:S(2)}) async-start(), calls=%async_computation.4 | async-start | bytes 2162688 | tf_op jit(solution)/shard_map/all_gather | solution.py:144
  9.3 857.7 %reduce-scatter.2.cloned.1.call-start = ((), (), s32[]{:S(2)}) async-start(), calls=%async_computation.5 | async-start | bytes 9437184 | tf_op jit(solution)/shard_map/reduce_scatter | solution.py:147
  258.1 14.0 %collective-permute-start = (f32[8,128,64]{2,1,0:T(8,128)}, f32[8,128,64]{2,1,0:T(8,128)S(1)}, u32[]{:S(2)}, u32[]{:S(2)}) collective-permute-start(f32[8,128,64]{2,1,0:T(8,128)} %multiply_add_fusion.2), channel_id=1, source_target_pairs={{0,8},{8,16},{16,24},{24,32},{32,40},{40,48},{48,56},{56,64},{64,7... | collective-permute-start | bytes 786440 | tf_op jit(solution)/shard_map/while/body/eval_jaxpr/ppermute | solution.py:12
  273.0 15.6 %collective-permute-start = (f32[8,128,64]{2,1,0:T(8,128)}, f32[8,128,64]{2,1,0:T(8,128)S(1)}, u32[]{:S(2)}, u32[]{:S(2)}) collective-permute-start(f32[8,128,64]{2,1,0:T(8,128)} %multiply_add_fusion.2), channel_id=1, source_target_pairs={{0,8},{8,16},{16,24},{24,32},{32,40},{40,48},{48,56},{56,64},{64,7... | collective-permute-start | bytes 786440 | tf_op jit(solution)/shard_map/while/body/eval_jaxpr/ppermute | solution.py:12
  325.9 13.3 %collective-permute-start = (f32[8,128,64]{2,1,0:T(8,128)}, f32[8,128,64]{2,1,0:T(8,128)S(1)}, u32[]{:S(2)}, u32[]{:S(2)}) collective-permute-start(f32[8,128,64]{2,1,0:T(8,128)} %multiply_add_fusion.2), channel_id=1, source_target_pairs={{0,8},{8,16},{16,24},{24,32},{32,40},{40,48},{48,56},{56,64},{64,7... | collective-permute-start | bytes 786440 | tf_op jit(solution)/shard_map/while/body/eval_jaxpr/ppermute | solution.py:12
  340.1 14.4 %collective-permute-start = (f32[8,128,64]{2,1,0:T(8,128)}, f32[8,128,64]{2,1,0:T(8,128)S(1)}, u32[]{:S(2)}, u32[]{:S(2)}) collective-permute-start(f32[8,128,64]{2,1,0:T(8,128)} %multiply_add_fusion.2), channel_id=1, source_target_pairs={{0,8},{8,16},{16,24},{24,32},{32,40},{40,48},{48,56},{56,64},{64,7... | collective-permute-start | bytes 786440 | tf_op jit(solution)/shard_map/while/body/eval_jaxpr/ppermute | solution.py:12
  355.4 15.6 %collective-permute-start = (f32[8,128,64]{2,1,0:T(8,128)}, f32[8,128,64]{2,1,0:T(8,128)S(1)}, u32[]{:S(2)}, u32[]{:S(2)}) collective-permute-start(f32[8,128,64]{2,1,0:T(8,128)} %multiply_add_fusion.2), channel_id=1, source_target_pairs={{0,8},{8,16},{16,24},{24,32},{32,40},{40,48},{48,56},{56,64},{64,7... | collective-permute-start | bytes 786440 | tf_op jit(solution)/shard_map/while/body/eval_jaxpr/ppermute | solution.py:12
  371.9 16.8 %collective-permute-start = (f32[8,128,64]{2,1,0:T(8,128)}, f32[8,128,64]{2,1,0:T(8,128)S(1)}, u32[]{:S(2)}, u32[]{:S(2)}) collective-permute-start(f32[8,128,64]{2,1,0:T(8,128)} %multiply_add_fusion.2), channel_id=1, source_target_pairs={{0,8},{8,16},{16,24},{24,32},{32,40},{40,48},{48,56},{56,64},{64,7... | collective-permute-start | bytes 786440 | tf_op jit(solution)/shard_map/while/body/eval_jaxpr/ppermute | solution.py:12
  389.6 16.3 %collective-permute-start = (f32[8,128,64]{2,1,0:T(8,128)}, f32[8,128,64]{2,1,0:T(8,128)S(1)}, u32[]{:S(2)}, u32[]{:S(2)}) collective-permute-start(f32[8,128,64]{2,1,0:T(8,128)} %multiply_add_fusion.2), channel_id=1, source_target_pairs={{0,8},{8,16},{16,24},{24,32},{32,40},{40,48},{48,56},{56,64},{64,7... | collective-permute-start | bytes 786440 | tf_op jit(solution)/shard_map/while/body/eval_jaxpr/ppermute | solution.py:12
  406.7 14.4 %collective-permute-start = (f32[8,128,64]{2,1,0:T(8,128)}, f32[8,128,64]{2,1,0:T(8,128)S(1)}, u32[]{:S(2)}, u32[]{:S(2)}) collective-permute-start(f32[8,128,64]{2,1,0:T(8,128)} %multiply_add_fusion.2), channel_id=1, source_target_pairs={{0,8},{8,16},{16,24},{24,32},{32,40},{40,48},{48,56},{56,64},{64,7... | collective-permute-start | bytes 786440 | tf_op jit(solution)/shard_map/while/body/eval_jaxpr/ppermute | solution.py:12
  422.1 12.7 %collective-permute-start = (f32[8,128,64]{2,1,0:T(8,128)}, f32[8,128,64]{2,1,0:T(8,128)S(1)}, u32[]{:S(2)}, u32[]{:S(2)}) collective-permute-start(f32[8,128,64]{2,1,0:T(8,128)} %multiply_add_fusion.2), channel_id=1, source_target_pairs={{0,8},{8,16},{16,24},{24,32},{32,40},{40,48},{48,56},{56,64},{64,7... | collective-permute-start | bytes 786440 | tf_op jit(solution)/shard_map/while/body/eval_jaxpr/ppermute | solution.py:12
  435.7 13.0 %collective-permute-start = (f32[8,128,64]{2,1,0:T(8,128)}, f32[8,128,64]{2,1,0:T(8,128)S(1)}, u32[]{:S(2)}, u32[]{:S(2)}) collective-permute-start(f32[8,128,64]{2,1,0:T(8,128)} %multiply_add_fusion.2), channel_id=1, source_target_pairs={{0,8},{8,16},{16,24},{24,32},{32,40},{40,48},{48,56},{56,64},{64,7... | collective-permute-start | bytes 786440 | tf_op jit(solution)/shard_map/while/body/eval_jaxpr/ppermute | solution.py:12
  513.5 13.7 %collective-permute-start = (f32[8,128,64]{2,1,0:T(8,128)}, f32[8,128,64]{2,1,0:T(8,128)S(1)}, u32[]{:S(2)}, u32[]{:S(2)}) collective-permute-start(f32[8,128,64]{2,1,0:T(8,128)} %multiply_add_fusion.2), channel_id=1, source_target_pairs={{0,8},{8,16},{16,24},{24,32},{32,40},{40,48},{48,56},{56,64},{64,7... | collective-permute-start | bytes 786440 | tf_op jit(solution)/shard_map/while/body/eval_jaxpr/ppermute | solution.py:12
  528.1 13.5 %collective-permute-start = (f32[8,128,64]{2,1,0:T(8,128)}, f32[8,128,64]{2,1,0:T(8,128)S(1)}, u32[]{:S(2)}, u32[]{:S(2)}) collective-permute-start(f32[8,128,64]{2,1,0:T(8,128)} %multiply_add_fusion.2), channel_id=1, source_target_pairs={{0,8},{8,16},{16,24},{24,32},{32,40},{40,48},{48,56},{56,64},{64,7... | collective-permute-start | bytes 786440 | tf_op jit(solution)/shard_map/while/body/eval_jaxpr/ppermute | solution.py:12
  542.5 15.6 %collective-permute-start = (f32[8,128,64]{2,1,0:T(8,128)}, f32[8,128,64]{2,1,0:T(8,128)S(1)}, u32[]{:S(2)}, u32[]{:S(2)}) collective-permute-start(f32[8,128,64]{2,1,0:T(8,128)} %multiply_add_fusion.2), channel_id=1, source_target_pairs={{0,8},{8,16},{16,24},{24,32},{32,40},{40,48},{48,56},{56,64},{64,7... | collective-permute-start | bytes 786440 | tf_op jit(solution)/shard_map/while/body/eval_jaxpr/ppermute | solution.py:12
  559.1 17.7 %collective-permute-start = (f32[8,128,64]{2,1,0:T(8,128)}, f32[8,128,64]{2,1,0:T(8,128)S(1)}, u32[]{:S(2)}, u32[]{:S(2)}) collective-permute-start(f32[8,128,64]{2,1,0:T(8,128)} %multiply_add_fusion.2), channel_id=1, source_target_pairs={{0,8},{8,16},{16,24},{24,32},{32,40},{40,48},{48,56},{56,64},{64,7... | collective-permute-start | bytes 786440 | tf_op jit(solution)/shard_map/while/body/eval_jaxpr/ppermute | solution.py:12
  577.7 19.4 %collective-permute-start = (f32[8,128,64]{2,1,0:T(8,128)}, f32[8,128,64]{2,1,0:T(8,128)S(1)}, u32[]{:S(2)}, u32[]{:S(2)}) collective-permute-start(f32[8,128,64]{2,1,0:T(8,128)} %multiply_add_fusion.2), channel_id=1, source_target_pairs={{0,8},{8,16},{16,24},{24,32},{32,40},{40,48},{48,56},{56,64},{64,7... | collective-permute-start | bytes 786440 | tf_op jit(solution)/shard_map/while/body/eval_jaxpr/ppermute | solution.py:12
  598.0 18.8 %collective-permute-start = (f32[8,128,64]{2,1,0:T(8,128)}, f32[8,128,64]{2,1,0:T(8,128)S(1)}, u32[]{:S(2)}, u32[]{:S(2)}) collective-permute-start(f32[8,128,64]{2,1,0:T(8,128)} %multiply_add_fusion.2), channel_id=1, source_target_pairs={{0,8},{8,16},{16,24},{24,32},{32,40},{40,48},{48,56},{56,64},{64,7... | collective-permute-start | bytes 786440 | tf_op jit(solution)/shard_map/while/body/eval_jaxpr/ppermute | solution.py:12
  617.7 16.6 %collective-permute-start = (f32[8,128,64]{2,1,0:T(8,128)}, f32[8,128,64]{2,1,0:T(8,128)S(1)}, u32[]{:S(2)}, u32[]{:S(2)}) collective-permute-start(f32[8,128,64]{2,1,0:T(8,128)} %multiply_add_fusion.2), channel_id=1, source_target_pairs={{0,8},{8,16},{16,24},{24,32},{32,40},{40,48},{48,56},{56,64},{64,7... | collective-permute-start | bytes 786440 | tf_op jit(solution)/shard_map/while/body/eval_jaxpr/ppermute | solution.py:12
  635.3 14.9 %collective-permute-start = (f32[8,128,64]{2,1,0:T(8,128)}, f32[8,128,64]{2,1,0:T(8,128)S(1)}, u32[]{:S(2)}, u32[]{:S(2)}) collective-permute-start(f32[8,128,64]{2,1,0:T(8,128)} %multiply_add_fusion.2), channel_id=1, source_target_pairs={{0,8},{8,16},{16,24},{24,32},{32,40},{40,48},{48,56},{56,64},{64,7... | collective-permute-start | bytes 786440 | tf_op jit(solution)/shard_map/while/body/eval_jaxpr/ppermute | solution.py:12
  651.1 12.9 %collective-permute-start = (f32[8,128,64]{2,1,0:T(8,128)}, f32[8,128,64]{2,1,0:T(8,128)S(1)}, u32[]{:S(2)}, u32[]{:S(2)}) collective-permute-start(f32[8,128,64]{2,1,0:T(8,128)} %multiply_add_fusion.2), channel_id=1, source_target_pairs={{0,8},{8,16},{16,24},{24,32},{32,40},{40,48},{48,56},{56,64},{64,7... | collective-permute-start | bytes 786440 | tf_op jit(solution)/shard_map/while/body/eval_jaxpr/ppermute | solution.py:12
  (35 other events, 1331.6 us)
Sparse Core Ops, SparseCore 0:
  9.9 75.0 all-gather.9
  86.8 41.0 all-gather.5
  130.5 78.7 all-gather.7
  211.7 75.2 all-gather.11
  793.5 73.4 reduce-scatter.1
where the time goes:
time: 878 us; the launch traced here: 876 us
  waiting for transfers between devices  483 us (55%)
  starting transfers between devices  162 us (18%)
  blocking collectives  90.2 us (10%)
  other arithmetic  68 us (8%)
  local copies, waits for them, and re-layouts  29.4 us (3%)
  matrix products  28.5 us (3%)
  between operations  13.5 us (2%)
    ppermute x33, waiting for transfers between devices, passed_along(): return lax.ppermute(value, axis, pairs)  270 us
    ppermute x33, starting transfers between devices, passed_along(): return lax.ppermute(value, axis, pairs)  162 us
    reduce_scatter x1, waiting for transfers between devices, on_device(): lax.psum_scatter(partial_out, 'tp', scatter_dimension=1, tiled=True)  72.8 us
    all_gather x1, waiting for transfers between devices, on_device(): lax.all_gather(w_inner, 'seq', axis=0, tiled=True)  67.3 us
    psum x1, blocking collectives, on_device(): squares = lax.psum(jnp.sum(gated * gated, axis=1), 'tp')  48.3 us
    all_gather x1, waiting for transfers between devices, on_device(): whole = lax.all_gather(tokens, 'tp', axis=1, tiled=True)  42.9 us
    all_gather x1, blocking collectives, on_device(): lax.all_gather(w_step, 'seq', axis=0, tiled=True)  41.9 us
    add x31, other arithmetic, relay(): block_gain[:, None, None] * entering_now + block_state  28.2 us
  transfers between devices with their start and end apart: 38, of which 35 were waited for; matrix products, arithmetic and copies ran while one was open for 13% of the time, Pallas kernels for 0%

commit v1 on v0

--- a/solution.py
+++ b/solution.py
@@ -61,7 +61,21 @@
     local_valid = lax.dynamic_slice_in_dim(valid_rows, seq_index * local_blocks, local_blocks)
     in_block = jnp.arange(row_count, dtype=jnp.int32) % BLOCK
     carry_on = jnp.repeat(local_start == 0, BLOCK)
-    whole = lax.all_gather(tokens, "tp", axis=1, tiled=True)
+    low, extra, item_now = (lax.axis_size("tp"), lax.axis_index("tp"), tokens.shape[1])
+    runs = [(j0, (j0 + 1) % low) for j0 in range(low)]
+    whole = jnp.zeros((*tokens.shape[:1], low * item_now, *tokens.shape[2:]), tokens.dtype)
+    whole = lax.dynamic_update_slice_in_dim(whole, tokens, extra * item_now, axis=1)
+    parts_seen = [(j0, (j0 - 1) % low) for j0 in range(low)]
+    v_now = tile_out = tokens
+    b_now = low // 2
+    for j in range(1, b_now + 1):
+        v_now = lax.ppermute(v_now, "tp", perm=runs)
+        whole = lax.dynamic_update_slice_in_dim(whole, v_now, (extra - j) % low * item_now, axis=1)
+        if j < low - b_now:
+            tile_out = lax.ppermute(tile_out, "tp", parts_seen)
+            whole = lax.dynamic_update_slice_in_dim(
+                whole, tile_out, (extra + j) % low * item_now, axis=1
+            )
     pieces = (
         lax.all_gather(w_inner, "seq", axis=0, tiled=True),
         lax.all_gather(w_states, "seq", axis=0, tiled=True),

time: 878 us -> 841 us (0.958)
  waiting for transfers between devices: 483 us -> 414 us
  starting transfers between devices: 162 us -> 182 us
  local copies, waits for them, and re-layouts: 29.4 us -> 38.2 us
    all_gather x1 -> x0, waiting for transfers between devices: 42.9 us -> none  [on_device(): whole = lax.all_gather(tokens, 'tp', axis=1, tiled=True)]
    all_gather x1, waiting for transfers between devices: 27.5 us -> 0.01 us  [on_device(): lax.all_gather(w_states, 'seq', axis=0, tiled=True)]
    ppermute x0 -> x7, starting transfers between devices: none -> 22.2 us  [the longest x3 14.7 us: on_device(): tile_out = lax.ppermute(tile_out, 'tp', parts_seen)]
    all_gather x1, waiting for transfers between devices: 67.3 us -> 57.5 us  [on_device(): lax.all_gather(w_inner, 'seq', axis=0, tiled=True)]
    ppermute x0 -> x7, waiting for transfers between devices: none -> 8.92 us  [the longest x4 7.38 us: on_device(): v_now = lax.ppermute(v_now, 'tp', perm=runs)]
  transfers between devices with their start and end apart: 38 -> 44, of which waited for: 35 -> 37; matrix products, arithmetic and copies ran while one was open for 13% -> 15% of each run, Pallas kernels for 0% -> 0%
where the time goes in v1:
time: 841 us; the launch traced here: 839 us
  waiting for transfers between devices  414 us (49%)
  starting transfers between devices  182 us (22%)
  blocking collectives  89.9 us (11%)
  other arithmetic  68.2 us (8%)
  local copies, waits for them, and re-layouts  38.2 us (5%)
  matrix products  32.7 us (4%)
  between operations  13.6 us (2%)
    ppermute x33, waiting for transfers between devices, passed_along(): return lax.ppermute(value, axis, pairs)  272 us
    ppermute x33, starting transfers between devices, passed_along(): return lax.ppermute(value, axis, pairs)  159 us
    reduce_scatter x1, waiting for transfers between devices, on_device(): lax.psum_scatter(partial_out, 'tp', scatter_dimension=1, tiled=True)  73.8 us
    all_gather x1, waiting for transfers between devices, on_device(): lax.all_gather(w_inner, 'seq', axis=0, tiled=True)  57.5 us
    psum x1, blocking collectives, on_device(): squares = lax.psum(jnp.sum(gated * gated, axis=1), 'tp')  48.9 us
    all_gather x1, blocking collectives, on_device(): lax.all_gather(w_step, 'seq', axis=0, tiled=True)  40.9 us
    add x31, other arithmetic, relay(): block_gain[:, None, None] * entering_now + block_state  28.2 us
  transfers between devices with their start and end apart: 44, of which 37 were waited for; matrix products, arithmetic and copies ran while one was open for 15% of the time, Pallas kernels for 0%

profile of v1, /device:TPU:1, one launch (start us, length us, event | category | flops | bytes accessed | tf_op | source)
XLA Modules:
  0.0 839.0 jit_solution(11360892853145548981)
XLA Ops:
  28.3 40.9 %all-gather = bf16[32,64,8]{1,2,0:T(8,128)(2,1)S(1)} all-gather(bf16[1,64,8]{1,2,0:T(8,128)(2,1)} %bitcast.99), channel_id=1, replica_groups=mesh['seq'=32,'tp'=8] {'seq'}, dimensions={0}, use_global_device_ids=true | all-gather | bytes 33792 | tf_op jit(solution)/shard_map/all_gather | solution.py:82
  74.9 12.4 %collective-permute-start.6 = (bf16[1024,256]{1,0:T(8,128)(2,1)S(1)}, bf16[1024,256]{1,0:T(8,128)(2,1)S(1)}, u32[]{:S(2)}, u32[]{:S(2)}) collective-permute-start(bf16[1024,256]{1,0:T(8,128)(2,1)S(1)} %collective-permute-done.4), channel_id=1, source_target_pairs={{0,7},{1,0},{2,1},{3,2},{4,3},{5,4},{6,5},{7,6},{8,15},{9,8},{10,9... | collective-permute-start | bytes 1572872 | tf_op jit(solution)/shard_map/ppermute | solution.py:75
  110.8 57.5 %all-gather.5.cloned.1.call-done = bf16[2048,2,512]{2,1,0:T(2,128)(2,1)} async-done(((bf16[64,2,512]{2,1,0:T(2,128)(2,1)}), bf16[2048,2,512]{2,1,0:T(2,128)(2,1)}) %all-gather.5.cloned.1.call-update) | async-done | bytes 4194320 | tf_op jit(solution)/shard_map/all_gather | solution.py:80
  207.1 454.8 %while.35 = (s32[]{:T(128)}, f32[8,128,64]{2,1,0:T(8,128)S(1)}, f32[8]{0:T(128)S(1)}, f32[8,128,64]{2,1,0:T(8,128)S(1)}, s32[]{:T(128)}) while((s32[]{:T(128)}, f32[8,128,64]{2,1,0:T(8,128)S(1)}, f32[8]{0:T(128)S(1)}, f32[8,128,64]{2,1,0:T(8,128)S(1)}, s32[]{:T(128)}) %tuple.77), condition=%wide.region_7.8_spmd, body=%wide.region_6.7_spmd.sunk | while | flops 131074 | bytes 1835141 | solution.py:137
  224.1 11.4 %collective-permute-done = f32[8,128,64]{2,1,0:T(8,128)S(1)} collective-permute-done((f32[8,128,64]{2,1,0:T(8,128)}, f32[8,128,64]{2,1,0:T(8,128)S(1)}, u32[]{:S(2)}, u32[]{:S(2)}) %collective-permute-start) | collective-permute-done | bytes 262176 | tf_op jit(solution)/shard_map/while/body/eval_jaxpr/ppermute | solution.py:12
  240.4 9.8 %collective-permute-done = f32[8,128,64]{2,1,0:T(8,128)S(1)} collective-permute-done((f32[8,128,64]{2,1,0:T(8,128)}, f32[8,128,64]{2,1,0:T(8,128)S(1)}, u32[]{:S(2)}, u32[]{:S(2)}) %collective-permute-start) | collective-permute-done | bytes 262176 | tf_op jit(solution)/shard_map/while/body/eval_jaxpr/ppermute | solution.py:12
  279.4 9.7 %collective-permute-done = f32[8,128,64]{2,1,0:T(8,128)S(1)} collective-permute-done((f32[8,128,64]{2,1,0:T(8,128)}, f32[8,128,64]{2,1,0:T(8,128)S(1)}, u32[]{:S(2)}, u32[]{:S(2)}) %collective-permute-start) | collective-permute-done | bytes 262176 | tf_op jit(solution)/shard_map/while/body/eval_jaxpr/ppermute | solution.py:12
  294.4 10.9 %collective-permute-done = f32[8,128,64]{2,1,0:T(8,128)S(1)} collective-permute-done((f32[8,128,64]{2,1,0:T(8,128)}, f32[8,128,64]{2,1,0:T(8,128)S(1)}, u32[]{:S(2)}, u32[]{:S(2)}) %collective-permute-start) | collective-permute-done | bytes 262176 | tf_op jit(solution)/shard_map/while/body/eval_jaxpr/ppermute | solution.py:12
  310.3 11.8 %collective-permute-done = f32[8,128,64]{2,1,0:T(8,128)S(1)} collective-permute-done((f32[8,128,64]{2,1,0:T(8,128)}, f32[8,128,64]{2,1,0:T(8,128)S(1)}, u32[]{:S(2)}, u32[]{:S(2)}) %collective-permute-start) | collective-permute-done | bytes 262176 | tf_op jit(solution)/shard_map/while/body/eval_jaxpr/ppermute | solution.py:12
  327.1 11.3 %collective-permute-done = f32[8,128,64]{2,1,0:T(8,128)S(1)} collective-permute-done((f32[8,128,64]{2,1,0:T(8,128)}, f32[8,128,64]{2,1,0:T(8,128)S(1)}, u32[]{:S(2)}, u32[]{:S(2)}) %collective-permute-start) | collective-permute-done | bytes 262176 | tf_op jit(solution)/shard_map/while/body/eval_jaxpr/ppermute | solution.py:12
  344.2 10.8 %collective-permute-done = f32[8,128,64]{2,1,0:T(8,128)S(1)} collective-permute-done((f32[8,128,64]{2,1,0:T(8,128)}, f32[8,128,64]{2,1,0:T(8,128)S(1)}, u32[]{:S(2)}, u32[]{:S(2)}) %collective-permute-start) | collective-permute-done | bytes 262176 | tf_op jit(solution)/shard_map/while/body/eval_jaxpr/ppermute | solution.py:12
  360.5 9.7 %collective-permute-done = f32[8,128,64]{2,1,0:T(8,128)S(1)} collective-permute-done((f32[8,128,64]{2,1,0:T(8,128)}, f32[8,128,64]{2,1,0:T(8,128)S(1)}, u32[]{:S(2)}, u32[]{:S(2)}) %collective-permute-start) | collective-permute-done | bytes 262176 | tf_op jit(solution)/shard_map/while/body/eval_jaxpr/ppermute | solution.py:12
  375.4 8.6 %collective-permute-done = f32[8,128,64]{2,1,0:T(8,128)S(1)} collective-permute-done((f32[8,128,64]{2,1,0:T(8,128)}, f32[8,128,64]{2,1,0:T(8,128)S(1)}, u32[]{:S(2)}, u32[]{:S(2)}) %collective-permute-start) | collective-permute-done | bytes 262176 | tf_op jit(solution)/shard_map/while/body/eval_jaxpr/ppermute | solution.py:12
  468.2 8.3 collective-permute-done
  483.3 9.5 %collective-permute-done = f32[8,128,64]{2,1,0:T(8,128)S(1)} collective-permute-done((f32[8,128,64]{2,1,0:T(8,128)}, f32[8,128,64]{2,1,0:T(8,128)S(1)}, u32[]{:S(2)}, u32[]{:S(2)}) %collective-permute-start) | collective-permute-done | bytes 262176 | tf_op jit(solution)/shard_map/while/body/eval_jaxpr/ppermute | solution.py:12
  498.7 10.2 %collective-permute-done = f32[8,128,64]{2,1,0:T(8,128)S(1)} collective-permute-done((f32[8,128,64]{2,1,0:T(8,128)}, f32[8,128,64]{2,1,0:T(8,128)S(1)}, u32[]{:S(2)}, u32[]{:S(2)}) %collective-permute-start) | collective-permute-done | bytes 262176 | tf_op jit(solution)/shard_map/while/body/eval_jaxpr/ppermute | solution.py:12
  515.2 11.1 %collective-permute-done = f32[8,128,64]{2,1,0:T(8,128)S(1)} collective-permute-done((f32[8,128,64]{2,1,0:T(8,128)}, f32[8,128,64]{2,1,0:T(8,128)S(1)}, u32[]{:S(2)}, u32[]{:S(2)}) %collective-permute-start) | collective-permute-done | bytes 262176 | tf_op jit(solution)/shard_map/while/body/eval_jaxpr/ppermute | solution.py:12
  532.0 11.6 %collective-permute-done = f32[8,128,64]{2,1,0:T(8,128)S(1)} collective-permute-done((f32[8,128,64]{2,1,0:T(8,128)}, f32[8,128,64]{2,1,0:T(8,128)S(1)}, u32[]{:S(2)}, u32[]{:S(2)}) %collective-permute-start) | collective-permute-done | bytes 262176 | tf_op jit(solution)/shard_map/while/body/eval_jaxpr/ppermute | solution.py:12
  552.4 11.3 %collective-permute-done = f32[8,128,64]{2,1,0:T(8,128)S(1)} collective-permute-done((f32[8,128,64]{2,1,0:T(8,128)}, f32[8,128,64]{2,1,0:T(8,128)S(1)}, u32[]{:S(2)}, u32[]{:S(2)}) %collective-permute-start) | collective-permute-done | bytes 262176 | tf_op jit(solution)/shard_map/while/body/eval_jaxpr/ppermute | solution.py:12
  571.5 10.1 %collective-permute-done = f32[8,128,64]{2,1,0:T(8,128)S(1)} collective-permute-done((f32[8,128,64]{2,1,0:T(8,128)}, f32[8,128,64]{2,1,0:T(8,128)S(1)}, u32[]{:S(2)}, u32[]{:S(2)}) %collective-permute-start) | collective-permute-done | bytes 262176 | tf_op jit(solution)/shard_map/while/body/eval_jaxpr/ppermute | solution.py:12
  588.7 9.0 %collective-permute-done = f32[8,128,64]{2,1,0:T(8,128)S(1)} collective-permute-done((f32[8,128,64]{2,1,0:T(8,128)}, f32[8,128,64]{2,1,0:T(8,128)S(1)}, u32[]{:S(2)}, u32[]{:S(2)}) %collective-permute-start) | collective-permute-done | bytes 262176 | tf_op jit(solution)/shard_map/while/body/eval_jaxpr/ppermute | solution.py:12
  661.9 15.3 %while.36 = (s32[]{:T(128)}, f32[8,128,64]{2,1,0:T(8,128)S(1)}, bf16[4,8,128,64]{3,2,1,0:T(8,128)(2,1)}, f32[4,8]{1,0:T(4,128)S(1)}, f32[4]{0:T(128)S(1)}, /*index=5*/f32[4,8,128,64]{3,2,1,0:T(8,128)}, s32[]{:T(128)}) while((s32[]{:T(128)}, f32[8,128,64]{2,1,0:T(8,128)S(1)}, bf16[4,8,128,64]{3,2,1,0:T(8,128)(2,1)}, f32[4,8]{1,0:T(4,128)S(1)}, ...), condition=%wide.region_9.10_spmd, body=%wide.region_8.9_spmd.sunk | while | flops 262146 | bytes 1574085 | solution.py:144
  698.6 48.9 %psum.7 = f32[1024]{0:T(1024)S(1)} all-reduce(f32[1024]{0:T(1024)S(1)} %get-tuple-element.196), channel_id=1, replica_groups=mesh['seq'=32,'tp'=8] {'tp'}, use_global_device_ids=true, to_apply=%region_11.12 | all-reduce | flops 1024 | bytes 8192 | tf_op jit(solution)/shard_map/psum | solution.py:153
  756.4 73.8 %reduce-scatter.2.cloned.1.call-done = f32[1024,256]{1,0:T(8,128)} async-done(((f32[1024,2048]{1,0:T(8,128)}), f32[1024,256]{1,0:T(8,128)}) %reduce-scatter.2.cloned.1.call-update) | async-done | bytes 1048592 | tf_op jit(solution)/shard_map/reduce_scatter | solution.py:161
  (244 shorter events, 423.7 us)
Async XLA Ops:
  6.5 88.7 %all-gather.7.cloned.1.call-start = ((), (), s32[]{:S(2)}) async-start(), calls=%async_computation.2 | async-start | bytes 1081344 | tf_op jit(solution)/shard_map/all_gather | solution.py:81
  7.3 161.1 %all-gather.5.cloned.1.call-start = ((), (), s32[]{:S(2)}) async-start(), calls=%async_computation.1 | async-start | bytes 4325376 | tf_op jit(solution)/shard_map/all_gather | solution.py:80
  8.0 739.6 %all-gather.9.cloned.1.call-start = ((), (), s32[]{:S(2)}) async-start(), calls=%async_computation.3 | async-start | bytes 2162688 | tf_op jit(solution)/shard_map/all_gather | solution.py:158
  11.3 818.9 %reduce-scatter.2.cloned.1.call-start = ((), (), s32[]{:S(2)}) async-start(), calls=%async_computation.4 | async-start | bytes 9437184 | tf_op jit(solution)/shard_map/reduce_scatter | solution.py:161
  20.4 54.5 %collective-permute-start.4 = (bf16[1024,256]{1,0:T(8,128)(2,1)S(1)}, bf16[1024,256]{1,0:T(8,128)(2,1)S(1)}, u32[]{:S(2)}, u32[]{:S(2)}) collective-permute-start(bf16[1024,256]{1,0:T(8,128)(2,1)S(1)} %collective-permute-done.2), channel_id=1, source_target_pairs={{0,7},{1,0},{2,1},{3,2},{4,3},{5,4},{6,5},{7,6},{8,15},{9,8},{10,9... | collective-permute-start | bytes 1572872 | tf_op jit(solution)/shard_map/ppermute | solution.py:75
  25.7 62.5 %collective-permute-start.5 = (bf16[1024,256]{1,0:T(8,128)(2,1)S(1)}, bf16[1024,256]{1,0:T(8,128)(2,1)S(1)}, u32[]{:S(2)}, u32[]{:S(2)}) collective-permute-start(bf16[1024,256]{1,0:T(8,128)(2,1)S(1)} %collective-permute-done.3), channel_id=1, source_target_pairs={{0,1},{1,2},{2,3},{3,4},{4,5},{5,6},{6,7},{7,0},{8,9},{9,10},{10,1... | collective-permute-start | bytes 1572872 | tf_op jit(solution)/shard_map/ppermute | solution.py:72
  74.9 18.3 %collective-permute-start.6 = (bf16[1024,256]{1,0:T(8,128)(2,1)S(1)}, bf16[1024,256]{1,0:T(8,128)(2,1)S(1)}, u32[]{:S(2)}, u32[]{:S(2)}) collective-permute-start(bf16[1024,256]{1,0:T(8,128)(2,1)S(1)} %collective-permute-done.4), channel_id=1, source_target_pairs={{0,7},{1,0},{2,1},{3,2},{4,3},{5,4},{6,5},{7,6},{8,15},{9,8},{10,9... | collective-permute-start | bytes 1572872 | tf_op jit(solution)/shard_map/ppermute | solution.py:75
  220.0 15.4 %collective-permute-start = (f32[8,128,64]{2,1,0:T(8,128)}, f32[8,128,64]{2,1,0:T(8,128)S(1)}, u32[]{:S(2)}, u32[]{:S(2)}) collective-permute-start(f32[8,128,64]{2,1,0:T(8,128)} %multiply_add_fusion.2), channel_id=1, source_target_pairs={{0,8},{8,16},{16,24},{24,32},{32,40},{40,48},{48,56},{56,64},{64,7... | collective-permute-start | bytes 786440 | tf_op jit(solution)/shard_map/while/body/eval_jaxpr/ppermute | solution.py:12
  236.3 13.8 %collective-permute-start = (f32[8,128,64]{2,1,0:T(8,128)}, f32[8,128,64]{2,1,0:T(8,128)S(1)}, u32[]{:S(2)}, u32[]{:S(2)}) collective-permute-start(f32[8,128,64]{2,1,0:T(8,128)} %multiply_add_fusion.2), channel_id=1, source_target_pairs={{0,8},{8,16},{16,24},{24,32},{32,40},{40,48},{48,56},{56,64},{64,7... | collective-permute-start | bytes 786440 | tf_op jit(solution)/shard_map/while/body/eval_jaxpr/ppermute | solution.py:12
  275.5 13.6 %collective-permute-start = (f32[8,128,64]{2,1,0:T(8,128)}, f32[8,128,64]{2,1,0:T(8,128)S(1)}, u32[]{:S(2)}, u32[]{:S(2)}) collective-permute-start(f32[8,128,64]{2,1,0:T(8,128)} %multiply_add_fusion.2), channel_id=1, source_target_pairs={{0,8},{8,16},{16,24},{24,32},{32,40},{40,48},{48,56},{56,64},{64,7... | collective-permute-start | bytes 786440 | tf_op jit(solution)/shard_map/while/body/eval_jaxpr/ppermute | solution.py:12
  290.0 15.2 %collective-permute-start = (f32[8,128,64]{2,1,0:T(8,128)}, f32[8,128,64]{2,1,0:T(8,128)S(1)}, u32[]{:S(2)}, u32[]{:S(2)}) collective-permute-start(f32[8,128,64]{2,1,0:T(8,128)} %multiply_add_fusion.2), channel_id=1, source_target_pairs={{0,8},{8,16},{16,24},{24,32},{32,40},{40,48},{48,56},{56,64},{64,7... | collective-permute-start | bytes 786440 | tf_op jit(solution)/shard_map/while/body/eval_jaxpr/ppermute | solution.py:12
  306.1 16.0 %collective-permute-start = (f32[8,128,64]{2,1,0:T(8,128)}, f32[8,128,64]{2,1,0:T(8,128)S(1)}, u32[]{:S(2)}, u32[]{:S(2)}) collective-permute-start(f32[8,128,64]{2,1,0:T(8,128)} %multiply_add_fusion.2), channel_id=1, source_target_pairs={{0,8},{8,16},{16,24},{24,32},{32,40},{40,48},{48,56},{56,64},{64,7... | collective-permute-start | bytes 786440 | tf_op jit(solution)/shard_map/while/body/eval_jaxpr/ppermute | solution.py:12
  323.0 15.4 %collective-permute-start = (f32[8,128,64]{2,1,0:T(8,128)}, f32[8,128,64]{2,1,0:T(8,128)S(1)}, u32[]{:S(2)}, u32[]{:S(2)}) collective-permute-start(f32[8,128,64]{2,1,0:T(8,128)} %multiply_add_fusion.2), channel_id=1, source_target_pairs={{0,8},{8,16},{16,24},{24,32},{32,40},{40,48},{48,56},{56,64},{64,7... | collective-permute-start | bytes 786440 | tf_op jit(solution)/shard_map/while/body/eval_jaxpr/ppermute | solution.py:12
  339.3 15.7 %collective-permute-start = (f32[8,128,64]{2,1,0:T(8,128)}, f32[8,128,64]{2,1,0:T(8,128)S(1)}, u32[]{:S(2)}, u32[]{:S(2)}) collective-permute-start(f32[8,128,64]{2,1,0:T(8,128)} %multiply_add_fusion.2), channel_id=1, source_target_pairs={{0,8},{8,16},{16,24},{24,32},{32,40},{40,48},{48,56},{56,64},{64,7... | collective-permute-start | bytes 786440 | tf_op jit(solution)/shard_map/while/body/eval_jaxpr/ppermute | solution.py:12
  355.9 14.3 %collective-permute-start = (f32[8,128,64]{2,1,0:T(8,128)}, f32[8,128,64]{2,1,0:T(8,128)S(1)}, u32[]{:S(2)}, u32[]{:S(2)}) collective-permute-start(f32[8,128,64]{2,1,0:T(8,128)} %multiply_add_fusion.2), channel_id=1, source_target_pairs={{0,8},{8,16},{16,24},{24,32},{32,40},{40,48},{48,56},{56,64},{64,7... | collective-permute-start | bytes 786440 | tf_op jit(solution)/shard_map/while/body/eval_jaxpr/ppermute | solution.py:12
  462.7 13.8 %collective-permute-start = (f32[8,128,64]{2,1,0:T(8,128)}, f32[8,128,64]{2,1,0:T(8,128)S(1)}, u32[]{:S(2)}, u32[]{:S(2)}) collective-permute-start(f32[8,128,64]{2,1,0:T(8,128)} %multiply_add_fusion.2), channel_id=1, source_target_pairs={{0,8},{8,16},{16,24},{24,32},{32,40},{40,48},{48,56},{56,64},{64,7... | collective-permute-start | bytes 786440 | tf_op jit(solution)/shard_map/while/body/eval_jaxpr/ppermute | solution.py:12
  477.4 15.3 %collective-permute-start = (f32[8,128,64]{2,1,0:T(8,128)}, f32[8,128,64]{2,1,0:T(8,128)S(1)}, u32[]{:S(2)}, u32[]{:S(2)}) collective-permute-start(f32[8,128,64]{2,1,0:T(8,128)} %multiply_add_fusion.2), channel_id=1, source_target_pairs={{0,8},{8,16},{16,24},{24,32},{32,40},{40,48},{48,56},{56,64},{64,7... | collective-permute-start | bytes 786440 | tf_op jit(solution)/shard_map/while/body/eval_jaxpr/ppermute | solution.py:12
  493.6 15.4 %collective-permute-start = (f32[8,128,64]{2,1,0:T(8,128)}, f32[8,128,64]{2,1,0:T(8,128)S(1)}, u32[]{:S(2)}, u32[]{:S(2)}) collective-permute-start(f32[8,128,64]{2,1,0:T(8,128)} %multiply_add_fusion.2), channel_id=1, source_target_pairs={{0,8},{8,16},{16,24},{24,32},{32,40},{40,48},{48,56},{56,64},{64,7... | collective-permute-start | bytes 786440 | tf_op jit(solution)/shard_map/while/body/eval_jaxpr/ppermute | solution.py:12
  509.9 16.5 %collective-permute-start = (f32[8,128,64]{2,1,0:T(8,128)}, f32[8,128,64]{2,1,0:T(8,128)S(1)}, u32[]{:S(2)}, u32[]{:S(2)}) collective-permute-start(f32[8,128,64]{2,1,0:T(8,128)} %multiply_add_fusion.2), channel_id=1, source_target_pairs={{0,8},{8,16},{16,24},{24,32},{32,40},{40,48},{48,56},{56,64},{64,7... | collective-permute-start | bytes 786440 | tf_op jit(solution)/shard_map/while/body/eval_jaxpr/ppermute | solution.py:12
  527.3 16.3 %collective-permute-start = (f32[8,128,64]{2,1,0:T(8,128)}, f32[8,128,64]{2,1,0:T(8,128)S(1)}, u32[]{:S(2)}, u32[]{:S(2)}) collective-permute-start(f32[8,128,64]{2,1,0:T(8,128)} %multiply_add_fusion.2), channel_id=1, source_target_pairs={{0,8},{8,16},{16,24},{24,32},{32,40},{40,48},{48,56},{56,64},{64,7... | collective-permute-start | bytes 786440 | tf_op jit(solution)/shard_map/while/body/eval_jaxpr/ppermute | solution.py:12
  544.5 19.2 %collective-permute-start = (f32[8,128,64]{2,1,0:T(8,128)}, f32[8,128,64]{2,1,0:T(8,128)S(1)}, u32[]{:S(2)}, u32[]{:S(2)}) collective-permute-start(f32[8,128,64]{2,1,0:T(8,128)} %multiply_add_fusion.2), channel_id=1, source_target_pairs={{0,8},{8,16},{16,24},{24,32},{32,40},{40,48},{48,56},{56,64},{64,7... | collective-permute-start | bytes 786440 | tf_op jit(solution)/shard_map/while/body/eval_jaxpr/ppermute | solution.py:12
  564.6 17.1 %collective-permute-start = (f32[8,128,64]{2,1,0:T(8,128)}, f32[8,128,64]{2,1,0:T(8,128)S(1)}, u32[]{:S(2)}, u32[]{:S(2)}) collective-permute-start(f32[8,128,64]{2,1,0:T(8,128)} %multiply_add_fusion.2), channel_id=1, source_target_pairs={{0,8},{8,16},{16,24},{24,32},{32,40},{40,48},{48,56},{56,64},{64,7... | collective-permute-start | bytes 786440 | tf_op jit(solution)/shard_map/while/body/eval_jaxpr/ppermute | solution.py:12
  582.5 15.1 %collective-permute-start = (f32[8,128,64]{2,1,0:T(8,128)}, f32[8,128,64]{2,1,0:T(8,128)S(1)}, u32[]{:S(2)}, u32[]{:S(2)}) collective-permute-start(f32[8,128,64]{2,1,0:T(8,128)} %multiply_add_fusion.2), channel_id=1, source_target_pairs={{0,8},{8,16},{16,24},{24,32},{32,40},{40,48},{48,56},{56,64},{64,7... | collective-permute-start | bytes 786440 | tf_op jit(solution)/shard_map/while/body/eval_jaxpr/ppermute | solution.py:12
  598.5 13.4 %collective-permute-start = (f32[8,128,64]{2,1,0:T(8,128)}, f32[8,128,64]{2,1,0:T(8,128)S(1)}, u32[]{:S(2)}, u32[]{:S(2)}) collective-permute-start(f32[8,128,64]{2,1,0:T(8,128)} %multiply_add_fusion.2), channel_id=1, source_target_pairs={{0,8},{8,16},{16,24},{24,32},{32,40},{40,48},{48,56},{56,64},{64,7... | collective-permute-start | bytes 786440 | tf_op jit(solution)/shard_map/while/body/eval_jaxpr/ppermute | solution.py:12
  (43 other events, 1029.3 us)
Sparse Core Ops, SparseCore 0:
  9.9 75.1 all-gather.6
  87.7 80.6 all-gather.4
  171.0 75.2 all-gather.8
  755.6 74.5 reduce-scatter.1
